TPU v7x, 32 devices: a whole 2x2x4 slice. The times are simulated.
32 devices in a mesh: blk: 4 (over y, x), group: 8 (over z, core).
Axes of the slice: x: 2, y: 2, z: 4, core: 2. Of those that a mesh axis runs over, the one named last changes fastest.
Arguments:
- picture_vector_list: bfloat16 [8, 1024, 768], P('group', 'blk'), may hold values from -0.25 to 0.25
- caption_latent_matrix: bfloat16 [8, 1024, 3072], P('group', 'blk'), may hold values from -6 to 6
- linear_map_matrix: bfloat16 [3072, 768], P('group'), may hold values from -0.109375 to 0.109375
- target_match_index: int32 [8, 1024], P('group', 'blk'), may hold values from 0 to 1023, each once within a row
- sharpness_factor: float32 [1], replicated, may hold values from 24 to 40
- offset_term: float32 [1], replicated, may hold values from -6 to -5
Outputs:
- row_loss: float32 [8, 1024], P('group', 'blk')
- image_grad: bfloat16 [8, 1024, 768], P('group', 'blk')
- projection_grad: float32 [3072, 768], P(('blk', 'group'))
Inputs may be any that keep to these rules, and one draw needn't show every extreme that they name: `target_match_index`: each data group's row of positives is a permutation of 0 to 1023.
All inputs are finite; a program needn't handle non-finite values.
Results may differ from a plain program's by a relative error of at most 0.015.
Values may be sent and summed in bfloat16 or wider, within the bound.
No kernel may reach another device: no remote copies, remote signals or barrier semaphores. Data moves between devices by JAX's collectives and lax.ppermute only.
A program may use at most 64 MiB of HBM per device.

v0:
```python
import jax
import jax.numpy as jnp
from jax import lax
from jax.sharding import PartitionSpec as P

epsilon = 1e-06


def passed_along(value, axis, steps):
    count = lax.axis_size(axis)
    pairs = [(source, (source + steps) % count) for source in range(count)]
    return lax.ppermute(value, axis, pairs)


def body(
    picture_vector_list,
    caption_latent_matrix,
    linear_map_matrix,
    target_match_index,
    sharpness_factor,
    offset_term,
):
    image_rows = picture_vector_list[0]
    hidden_rows = caption_latent_matrix[0]
    label_rows = target_match_index[0]
    row_count = image_rows.shape[0]
    feature_dim = image_rows.shape[1]
    blocks = lax.axis_size("blk")
    my_index = lax.axis_index("blk")
    multiplier_amount = sharpness_factor[0]
    offset_value = offset_term[0]
    columns = hidden_rows
    projected = jnp.dot(
        columns,
        lax.all_gather(linear_map_matrix, "group", axis=0, tiled=True),
        preferred_element_type=jnp.float32,
    )
    text_scale = lax.rsqrt(jnp.sum(projected * projected, axis=1, keepdims=True) + epsilon)
    text_dir = projected * text_scale
    text_unit = text_dir.astype(jnp.bfloat16)
    image_float = image_rows.astype(jnp.float32)
    image_scale = lax.rsqrt(jnp.sum(image_float * image_float, axis=1, keepdims=True) + epsilon)
    image_dir = image_float * image_scale
    image_unit = image_dir.astype(jnp.bfloat16)

    def signed_logits(image_tile_rows, label_block, text_block, column_start):
        columns = column_start + jnp.arange(text_block.shape[0], dtype=jnp.int32)
        pair_sign = jnp.where(label_block[:, None] == columns[None, :], 1.0, -1.0).astype(
            jnp.float32
        )
        pair_scores = lax.dot_general(
            image_tile_rows,
            text_block,
            (((1,), (1,)), ((), ())),
            preferred_element_type=jnp.float32,
        )
        return (multiplier_amount * pair_scores + offset_value, pair_sign)

    def weights_of(logits, pair_sign):
        return (-pair_sign * jax.nn.sigmoid(-pair_sign * logits) * multiplier_amount).astype(
            jnp.bfloat16
        )

    image_unit_grad = jnp.zeros((row_count, feature_dim), jnp.float32)
    loss_local = jnp.zeros((row_count,), jnp.float32)
    text_block = text_unit
    for step_index in range(blocks):
        source = (my_index - step_index) % blocks
        logits, pair_sign = signed_logits(image_unit, label_rows, text_block, source * row_count)
        loss_local = loss_local + -jnp.sum(jax.nn.log_sigmoid(pair_sign * logits), axis=1)
        pair_weight = weights_of(logits, pair_sign)
        image_unit_grad = image_unit_grad + jnp.dot(
            pair_weight, text_block, preferred_element_type=jnp.float32
        )
        if step_index + 1 < blocks:
            text_block = passed_along(text_block, "blk", 1)
    own_start = my_index * row_count
    image_piece = lax.all_gather(image_unit, "blk", axis=0, tiled=True)
    label_piece = lax.all_gather(label_rows, "blk", axis=0, tiled=True)
    logits, pair_sign = signed_logits(image_piece, label_piece, text_unit, own_start)
    pair_weight = weights_of(logits, pair_sign)
    text_unit_grad = lax.dot_general(
        pair_weight, image_piece, (((0,), (0,)), ((), ())), preferred_element_type=jnp.float32
    )
    image_grad = (
        image_scale
        * (
            image_unit_grad
            - image_dir * jnp.sum(image_dir * image_unit_grad, axis=1, keepdims=True)
        )
    ).astype(jnp.bfloat16)
    projection_output_gradient = (
        text_scale
        * (text_unit_grad - text_dir * jnp.sum(text_dir * text_unit_grad, axis=1, keepdims=True))
    ).astype(jnp.bfloat16)
    columns = hidden_rows
    projection_grad = lax.psum_scatter(
        lax.dot_general(
            columns,
            projection_output_gradient,
            (((0,), (0,)), ((), ())),
            preferred_element_type=jnp.float32,
        ),
        ("blk", "group"),
        scatter_dimension=0,
        tiled=True,
    )
    return (loss_local[None], image_grad[None], projection_grad)


def solution(mesh):
    return jax.shard_map(
        body,
        mesh=mesh,
        in_specs=(
            P("group", "blk", None),
            P("group", "blk", None),
            P("group", None),
            P("group", "blk"),
            P(),
            P(),
        ),
        out_specs=(P("group", "blk"), P("group", "blk", None), P(("blk", "group"), None)),
        check_vma=False,
    )
```

profile of v0, /device:TPU:0, one launch (start us, length us, event | category | flops | bytes accessed | tf_op | source)
XLA Modules:
  0.0 257.5 jit_solution(9647050227928517033)
XLA Ops:
  7.2 0.0 copy-start
  7.2 0.0 copy-start.3
  7.2 0.0 all-gather.4.cloned.1.call-start
  7.2 0.7 all-gather.4.cloned.1.call-update
  7.9 0.0 all-gather.6.cloned.1.call-start
  8.0 1.2 fusion.27
  9.1 1.9 fusion.22
  11.0 0.0 all-gather.6.cloned.1.call-update
  11.0 0.0 reduce-scatter.4.cloned.1.call-start
  12.4 0.0 copy-done.3
  12.4 10.1 %all-gather = s32[1,1024]{1,0:T(1,128)} all-gather(s32[1,256]{1,0:T(1,128)S(1)} %copy-done.3), channel_id=2, replica_groups=mesh['blk'=4,'group'=8] {'blk'}, dimensions={1}, use_global_device_ids=true | all-gather | bytes 5120 | tf_op jit(solution)/shard_map/all_gather | solution.py:79
  22.5 0.6 iota_add_fusion
  23.0 41.1 %all-gather.4.cloned.1.call-done = bf16[3072,768]{1,0:T(8,128)(2,1)} async-done(((bf16[384,768]{1,0:T(8,128)(2,1)}), bf16[3072,768]{1,0:T(8,128)(2,1)}) %all-gather.4.cloned.1.call-update) | async-done | bytes 4718608 | tf_op jit(solution)/shard_map/all_gather | solution.py:35
  64.1 0.0 copy-done
  64.1 3.8 %multiply_reduce_fusion.1 = (f32[256]{0:T(256)S(1)}, f32[256,768]{1,0:T(8,128)S(1)}) fusion(bf16[3072,768]{1,0:T(8,128)(2,1)} %all-gather.4.cloned.1.call-done, bf16[1,256,3072]{2,1,0:T(8,128)(2,1)S(1)} %copy-done), kind=kOutput, calls=%fused_computation.41 | convolution fusion | flops 1208352512 | bytes 7078912 | tf_op jit(solution)/shard_map/dot_general | solution.py:33
  67.9 0.1 multiply_convert_fusion.1
  68.0 28.3 %all-gather.6.cloned.1.call-done = bf16[1024,768]{1,0:T(8,128)(2,1)} async-done(((bf16[256,768]{1,0:T(8,128)(2,1)}), bf16[1024,768]{1,0:T(8,128)(2,1)}) %all-gather.6.cloned.1.call-update) | async-done | bytes 1572880 | tf_op jit(solution)/shard_map/all_gather | solution.py:78
  96.3 3.9 %multiply_reduce_fusion = (f32[256]{0:T(256)S(1)}, f32[256,768]{1,0:T(8,128)S(1)}) fusion(f32[256,768]{1,0:T(8,128)S(1)} %get-tuple-element.14, f32[256]{0:T(256)S(1)} %add_rsqrt_fusion, bf16[1024,768]{1,0:T(8,128)(2,1)} %all-gather.6.cloned.1.call-done, bf16[256,768]{1,0:T(8,128)(2,1)S(1)} %multiply_convert_fusion.1, f32[]{:T(128)} %bitcast.49, ...), kind=kOutput, calls=%fused_computation.40 | convolution fusion | flops 809041664 | bytes 3546120 | tf_op jit(solution)/shard_map/dot_general | solution.py:82
  100.2 5.3 %convolution_bitcast_fusion = f32[3072,768]{0,1:T(8,128)} fusion(bf16[1,256,3072]{2,1,0:T(8,128)(2,1)S(1)} %copy-done, f32[256,768]{1,0:T(8,128)S(1)} %get-tuple-element.19, f32[256,768]{1,0:T(8,128)S(1)} %get-tuple-element.14, f32[256]{0:T(256)S(1)} %get-tuple-element.18, f32[256]{0:T(256)S(1)} %add_rsqrt_fusion), kind=kOutput, calls=%fused_computation | convolution fusion | flops 1208942592 | bytes 12584960 | tf_op jit(solution)/shard_map/dot_general | solution.py:98
  105.5 9.6 %copy.11 = f32[3072,768]{1,0:T(8,128)} copy(f32[3072,768]{0,1:T(8,128)} %convolution_bitcast_fusion) | data formatting | bytes 18874368
  115.1 0.0 copy-start.1
  115.1 0.0 reduce-scatter.4.cloned.1.call-update
  115.2 1.5 collective-permute-start
  116.7 10.3 %collective-permute-done = bf16[256,768]{1,0:T(8,128)(2,1)S(1)} collective-permute-done((bf16[256,768]{1,0:T(8,128)(2,1)S(1)}, bf16[256,768]{1,0:T(8,128)(2,1)S(1)}, u32[]{:S(2)}, u32[]{:S(2)}) %collective-permute-start) | collective-permute-done | bytes 393248 | tf_op jit(solution)/shard_map/ppermute | solution.py:12
  127.0 0.6 collective-permute-start.1
  127.5 0.0 copy-done.1
  127.5 0.3 fusion.12
  127.8 10.0 %collective-permute-done.1 = bf16[256,768]{1,0:T(8,128)(2,1)S(1)} collective-permute-done((bf16[256,768]{1,0:T(8,128)(2,1)S(1)}, bf16[256,768]{1,0:T(8,128)(2,1)S(1)}, u32[]{:S(2)}, u32[]{:S(2)}) %collective-permute-start.1) | collective-permute-done | bytes 393248 | tf_op jit(solution)/shard_map/ppermute | solution.py:12
  137.8 0.0 collective-permute-start.2
  137.8 0.4 fusion.77
  138.3 0.3 fusion.14
  138.6 9.2 %collective-permute-done.2 = bf16[256,768]{1,0:T(8,128)(2,1)S(1)} collective-permute-done((bf16[256,768]{1,0:T(8,128)(2,1)S(1)}, bf16[256,768]{1,0:T(8,128)(2,1)S(1)}, u32[]{:S(2)}, u32[]{:S(2)}) %collective-permute-start.2) | collective-permute-done | bytes 393248 | tf_op jit(solution)/shard_map/ppermute | solution.py:12
  147.8 0.3 fusion.15
  148.1 0.9 fusion.70
  149.0 0.6 add_add_fusion
  149.6 0.4 convolution_add_fusion.2
  150.0 0.0 copy-start.2
  150.0 0.4 convolution_add_fusion.1
  150.5 0.5 copy-done.2
  151.0 0.5 fusion.23
  151.6 1.0 fusion.34
  152.5 98.5 %reduce-scatter.4.cloned.1.call-done = f32[96,768]{1,0:T(8,128)} async-done(((f32[3072,768]{1,0:T(8,128)}), f32[96,768]{1,0:T(8,128)}) %reduce-scatter.4.cloned.1.call-update) | async-done | bytes 294928
  (4 shorter events, 0.0 us)
Async XLA Ops:
  7.2 56.9 %copy-start = (bf16[1,256,3072]{2,1,0:T(8,128)(2,1)S(1)}, bf16[1,256,3072]{2,1,0:T(8,128)(2,1)}, u32[]{:S(2)}) copy-start(bf16[1,256,3072]{2,1,0:T(8,128)(2,1)} %param.7) | copy-start | bytes 4718596
  7.2 5.2 %copy-start.3 = (s32[1,256]{1,0:T(1,128)S(1)}, s32[1,256]{1,0:T(1,128)}, u32[]{:S(2)}) copy-start(s32[1,256]{1,0:T(1,128)} %param.9) | copy-start | bytes 3076
  7.2 56.9 %all-gather.4.cloned.1.call-start = ((), (), s32[]{:S(2)}) async-start(), calls=%async_computation.1 | async-start | bytes 5308416 | tf_op jit(solution)/shard_map/all_gather | solution.py:35
  7.9 88.4 %all-gather.6.cloned.1.call-start = ((), (), s32[]{:S(2)}) async-start(), calls=%async_computation.2 | async-start | bytes 1966080 | tf_op jit(solution)/shard_map/all_gather | solution.py:78
  11.0 240.0 %reduce-scatter.4.cloned.1.call-start = ((), (), s32[]{:S(2)}) async-start(), calls=%async_computation.3 | async-start | bytes 9732096
  115.1 12.4 %copy-start.1 = (bf16[256,768]{1,0:T(8,128)(2,1)S(1)}, bf16[256,768]{1,0:T(8,128)(2,1)}, u32[]{:S(2)}) copy-start(bf16[256,768]{1,0:T(8,128)(2,1)} %fusion.22) | copy-start | bytes 1179652
  115.2 11.8 %collective-permute-start = (bf16[256,768]{1,0:T(8,128)(2,1)S(1)}, bf16[256,768]{1,0:T(8,128)(2,1)S(1)}, u32[]{:S(2)}, u32[]{:S(2)}) collective-permute-start(bf16[256,768]{1,0:T(8,128)(2,1)S(1)} %multiply_convert_fusion.1), channel_id=1, source_target_pairs={{0,8},{8,16},{16,24},{24,0},{1,9},{9,17},{17,25},{25,1},{2,10},{10... | collective-permute-start | bytes 1179656 | tf_op jit(solution)/shard_map/ppermute | solution.py:12
  127.0 10.9 %collective-permute-start.1 = (bf16[256,768]{1,0:T(8,128)(2,1)S(1)}, bf16[256,768]{1,0:T(8,128)(2,1)S(1)}, u32[]{:S(2)}, u32[]{:S(2)}) collective-permute-start(bf16[256,768]{1,0:T(8,128)(2,1)S(1)} %collective-permute-done), channel_id=1, source_target_pairs={{0,8},{8,16},{16,24},{24,0},{1,9},{9,17},{17,25},{25,1},{2,10},{10... | collective-permute-start | bytes 1179656 | tf_op jit(solution)/shard_map/ppermute | solution.py:12
  137.8 10.0 %collective-permute-start.2 = (bf16[256,768]{1,0:T(8,128)(2,1)S(1)}, bf16[256,768]{1,0:T(8,128)(2,1)S(1)}, u32[]{:S(2)}, u32[]{:S(2)}) collective-permute-start(bf16[256,768]{1,0:T(8,128)(2,1)S(1)} %collective-permute-done.1), channel_id=1, source_target_pairs={{0,8},{8,16},{16,24},{24,0},{1,9},{9,17},{17,25},{25,1},{2,10},{10... | collective-permute-start | bytes 1179656 | tf_op jit(solution)/shard_map/ppermute | solution.py:12
  150.0 1.0 copy-start.2
Sparse Core Ops, SparseCore 0:
  9.7 54.3 all-gather.3
  66.5 29.7 all-gather.5
  115.3 135.6 reduce-scatter.3
where the time goes:
time: 258 us
  waiting for transfers between devices  198 us (77%)
  matrix products  16.6 us (6%)
  between operations  15.1 us (6%)
  local copies, waits for them, and re-layouts  10.2 us (4%)
  blocking collectives  10.1 us (4%)
  other arithmetic  5.28 us (2%)
    unnamed x4, waiting for transfers between devices  99.2 us
    all_gather x1, waiting for transfers between devices, body(): lax.all_gather(linear_map_matrix, 'group', axis=0, tiled=True)  41.1 us
    ppermute x3, waiting for transfers between devices, passed_along(): return lax.ppermute(value, axis, pairs)  29.5 us
    all_gather x1, waiting for transfers between devices, body(): image_piece = lax.all_gather(image_unit, 'blk', axis=0, tiled=True)  28.3 us
    unnamed x9, local copies, waits for them, and re-layouts  10.2 us
    all_gather x1, blocking collectives, body(): label_piece = lax.all_gather(label_rows, 'blk', axis=0, tiled=True)  10.1 us
    dot_general x1, matrix products, body(): lax.dot_general(columns, projection_output_gradient, (((0,), (0,)), ((),...  5.27 us
  transfers between devices with their start and end apart: 6, of which 6 were waited for; matrix products, arithmetic and copies ran while one was open for 5% of the time, Pallas kernels for 0%

commit v1 on v0

--- a/solution.py
+++ b/solution.py
@@ -76,7 +76,14 @@
             text_block = passed_along(text_block, "blk", 1)
     own_start = my_index * row_count
     image_piece = lax.all_gather(image_unit, "blk", axis=0, tiled=True)
-    label_piece = lax.all_gather(label_rows, "blk", axis=0, tiled=True)
+    ways, here, lap = (lax.axis_size("blk"), lax.axis_index("blk"), label_rows.shape[0])
+    line, have = (label_rows, 1)
+    while have < ways:
+        line = jnp.concatenate(
+            [line, lax.ppermute(line, "blk", [(d, (d - have) % ways) for d in range(ways)])], axis=0
+        )
+        have = 2 * have
+    label_piece = jnp.roll(line, here * lap, axis=0)
     logits, pair_sign = signed_logits(image_piece, label_piece, text_unit, own_start)
     pair_weight = weights_of(logits, pair_sign)
     text_unit_grad = lax.dot_general(

time: 258 us -> 258 us (level)
  blocking collectives: 10.1 us -> 0 us
  waiting for transfers between devices: 198 us -> 203 us
  starting transfers between devices: 2.2 us -> 6.9 us
    all_gather x1 -> x0, blocking collectives: 10.1 us -> none  [body(): label_piece = lax.all_gather(label_rows, 'blk', axis=0, tiled=True)]
    ppermute x0 -> x2, starting transfers between devices: none -> 4.7 us  [body(): lax.ppermute(line, 'blk', [(d, (d - have) % ways) for d in range(ways)])]
    ppermute x0 -> x2, waiting for transfers between devices: none -> 2.89 us  [body(): lax.ppermute(line, 'blk', [(d, (d - have) % ways) for d in range(ways)])]
    unnamed x9 -> x14, local copies, waits for them, and re-layouts: 10.2 us -> 10.2 us
  transfers between devices with their start and end apart: 6 -> 8, of which waited for: 6 -> 7; matrix products, arithmetic and copies ran while one was open for 5% -> 5% of each run, Pallas kernels for 0% -> 0%
where the time goes in v1:
time: 258 us; the launch traced here: 257 us
  waiting for transfers between devices  203 us (79%)
  matrix products  16.6 us (6%)
  between operations  15.2 us (6%)
  local copies, waits for them, and re-layouts  10.9 us (4%)
  starting transfers between devices  6.9 us (3%)
  other arithmetic  5.28 us (2%)
    unnamed x4, waiting for transfers between devices  99.2 us
    all_gather x1, waiting for transfers between devices, body(): lax.all_gather(linear_map_matrix, 'group', axis=0, tiled=True)  42.8 us
    ppermute x3, waiting for transfers between devices, passed_along(): return lax.ppermute(value, axis, pairs)  29.5 us
    all_gather x1, waiting for transfers between devices, body(): image_piece = lax.all_gather(image_unit, 'blk', axis=0, tiled=True)  28.3 us
    unnamed x14, local copies, waits for them, and re-layouts  10.2 us
    dot_general x1, matrix products, body(): lax.dot_general(columns, projection_output_gradient, (((0,), (0,)), ((),...  5.27 us
  transfers between devices with their start and end apart: 8, of which 7 were waited for; matrix products, arithmetic and copies ran while one was open for 5% of the time, Pallas kernels for 0%

profile of v1, /device:TPU:0, one launch (start us, length us, event | category | flops | bytes accessed | tf_op | source)
XLA Modules:
  0.0 257.5 jit_solution(6476372037910542621)
XLA Ops:
  7.2 0.0 copy-start
  7.2 0.0 copy-start.3
  7.2 0.0 all-gather.3.cloned.1.call-start
  7.2 0.7 all-gather.3.cloned.1.call-update
  7.9 0.0 all-gather.5.cloned.1.call-start
  8.0 1.2 fusion.27
  9.1 1.9 fusion.22
  11.0 0.0 all-gather.5.cloned.1.call-update
  11.0 0.0 reduce-scatter.4.cloned.1.call-start
  11.1 0.0 copy-done.3
  11.1 3.9 %collective-permute-start.3 = (s32[256]{0:T(256)S(1)}, s32[256]{0:T(256)S(1)}, u32[]{:S(2)}, u32[]{:S(2)}) collective-permute-start(s32[256]{0:T(256)S(1)} %bitcast.52), channel_id=1, source_target_pairs={{0,24},{8,0},{16,8},{24,16},{1,25},{9,1},{17,9},{25,17},{2,26},{10... | collective-permute-start | bytes 3080 | tf_op jit(solution)/shard_map/ppermute | solution.py:83
  15.0 0.6 iota_add_fusion
  16.9 0.0 collective-permute-done.3
  16.9 0.8 collective-permute-start.4
  17.7 2.9 %collective-permute-done.4 = s32[512]{0:T(512)S(1)} collective-permute-done((s32[512]{0:T(512)S(1)}, s32[512]{0:T(512)S(1)}, u32[]{:S(2)}, u32[]{:S(2)}) %collective-permute-start.4) | collective-permute-done | bytes 2080 | tf_op jit(solution)/shard_map/ppermute | solution.py:83
  20.6 0.7 dynamic_slice.4
  21.3 42.8 %all-gather.3.cloned.1.call-done = bf16[3072,768]{1,0:T(8,128)(2,1)} async-done(((bf16[384,768]{1,0:T(8,128)(2,1)}), bf16[3072,768]{1,0:T(8,128)(2,1)}) %all-gather.3.cloned.1.call-update) | async-done | bytes 4718608 | tf_op jit(solution)/shard_map/all_gather | solution.py:35
  64.1 0.0 copy-done
  64.1 3.8 %multiply_reduce_fusion.1 = (f32[256]{0:T(256)S(1)}, f32[256,768]{1,0:T(8,128)S(1)}) fusion(bf16[3072,768]{1,0:T(8,128)(2,1)} %all-gather.3.cloned.1.call-done, bf16[1,256,3072]{2,1,0:T(8,128)(2,1)S(1)} %copy-done), kind=kOutput, calls=%fused_computation.41 | convolution fusion | flops 1208352512 | bytes 7078912 | tf_op jit(solution)/shard_map/dot_general | solution.py:33
  67.9 0.1 multiply_convert_fusion.1
  68.0 28.3 %all-gather.5.cloned.1.call-done = bf16[1024,768]{1,0:T(8,128)(2,1)} async-done(((bf16[256,768]{1,0:T(8,128)(2,1)}), bf16[1024,768]{1,0:T(8,128)(2,1)}) %all-gather.5.cloned.1.call-update) | async-done | bytes 1572880 | tf_op jit(solution)/shard_map/all_gather | solution.py:78
  96.3 3.9 %multiply_reduce_fusion = (f32[256]{0:T(256)S(1)}, f32[256,768]{1,0:T(8,128)S(1)}) fusion(f32[256,768]{1,0:T(8,128)S(1)} %get-tuple-element.14, f32[256]{0:T(256)S(1)} %add_rsqrt_fusion, bf16[1024,768]{1,0:T(8,128)(2,1)} %all-gather.5.cloned.1.call-done, bf16[256,768]{1,0:T(8,128)(2,1)S(1)} %multiply_convert_fusion.1, f32[]{:T(128)} %bitcast.48, ...), kind=kOutput, calls=%fused_computation.40 | convolution fusion | flops 809041664 | bytes 3546120 | tf_op jit(solution)/shard_map/dot_general | solution.py:89
  100.2 5.3 %convolution_bitcast_fusion = f32[3072,768]{0,1:T(8,128)} fusion(bf16[1,256,3072]{2,1,0:T(8,128)(2,1)S(1)} %copy-done, f32[256,768]{1,0:T(8,128)S(1)} %get-tuple-element.19, f32[256,768]{1,0:T(8,128)S(1)} %get-tuple-element.14, f32[256]{0:T(256)S(1)} %get-tuple-element.18, f32[256]{0:T(256)S(1)} %add_rsqrt_fusion), kind=kOutput, calls=%fused_computation | convolution fusion | flops 1208942592 | bytes 12584960 | tf_op jit(solution)/shard_map/dot_general | solution.py:105
  105.5 9.6 %copy.11 = f32[3072,768]{1,0:T(8,128)} copy(f32[3072,768]{0,1:T(8,128)} %convolution_bitcast_fusion) | data formatting | bytes 18874368
  115.1 0.0 copy-start.1
  115.1 0.0 reduce-scatter.4.cloned.1.call-update
  115.2 1.5 collective-permute-start
  116.7 10.3 %collective-permute-done = bf16[256,768]{1,0:T(8,128)(2,1)S(1)} collective-permute-done((bf16[256,768]{1,0:T(8,128)(2,1)S(1)}, bf16[256,768]{1,0:T(8,128)(2,1)S(1)}, u32[]{:S(2)}, u32[]{:S(2)}) %collective-permute-start) | collective-permute-done | bytes 393248 | tf_op jit(solution)/shard_map/ppermute | solution.py:12
  127.0 0.6 collective-permute-start.1
  127.5 0.0 copy-done.1
  127.5 0.3 fusion.12
  127.8 10.0 %collective-permute-done.1 = bf16[256,768]{1,0:T(8,128)(2,1)S(1)} collective-permute-done((bf16[256,768]{1,0:T(8,128)(2,1)S(1)}, bf16[256,768]{1,0:T(8,128)(2,1)S(1)}, u32[]{:S(2)}, u32[]{:S(2)}) %collective-permute-start.1) | collective-permute-done | bytes 393248 | tf_op jit(solution)/shard_map/ppermute | solution.py:12
  137.8 0.0 collective-permute-start.2
  137.8 0.4 fusion.77
  138.3 0.3 fusion.14
  138.6 9.2 %collective-permute-done.2 = bf16[256,768]{1,0:T(8,128)(2,1)S(1)} collective-permute-done((bf16[256,768]{1,0:T(8,128)(2,1)S(1)}, bf16[256,768]{1,0:T(8,128)(2,1)S(1)}, u32[]{:S(2)}, u32[]{:S(2)}) %collective-permute-start.2) | collective-permute-done | bytes 393248 | tf_op jit(solution)/shard_map/ppermute | solution.py:12
  147.8 0.3 fusion.15
  148.1 0.9 fusion.70
  149.0 0.6 add_add_fusion
  149.6 0.4 convolution_add_fusion.2
  150.0 0.0 copy-start.2
  150.0 0.4 convolution_add_fusion.1
  150.5 0.5 copy-done.2
  151.0 0.5 fusion.23
  151.6 1.0 fusion.34
  152.5 98.4 %reduce-scatter.4.cloned.1.call-done = f32[96,768]{1,0:T(8,128)} async-done(((f32[3072,768]{1,0:T(8,128)}), f32[96,768]{1,0:T(8,128)}) %reduce-scatter.4.cloned.1.call-update) | async-done | bytes 294928
  (12 shorter events, 0.1 us)
Async XLA Ops:
  7.2 56.9 %copy-start = (bf16[1,256,3072]{2,1,0:T(8,128)(2,1)S(1)}, bf16[1,256,3072]{2,1,0:T(8,128)(2,1)}, u32[]{:S(2)}) copy-start(bf16[1,256,3072]{2,1,0:T(8,128)(2,1)} %param.7) | copy-start | bytes 4718596
  7.2 3.9 %copy-start.3 = (s32[1,256]{1,0:T(1,128)S(1)}, s32[1,256]{1,0:T(1,128)}, u32[]{:S(2)}) copy-start(s32[1,256]{1,0:T(1,128)} %param.9) | copy-start | bytes 3076
  7.2 56.9 %all-gather.3.cloned.1.call-start = ((), (), s32[]{:S(2)}) async-start(), calls=%async_computation.1 | async-start | bytes 5308416 | tf_op jit(solution)/shard_map/all_gather | solution.py:35
  7.9 88.4 %all-gather.5.cloned.1.call-start = ((), (), s32[]{:S(2)}) async-start(), calls=%async_computation.2 | async-start | bytes 1966080 | tf_op jit(solution)/shard_map/all_gather | solution.py:78
  11.0 239.9 %reduce-scatter.4.cloned.1.call-start = ((), (), s32[]{:S(2)}) async-start(), calls=%async_computation.3 | async-start | bytes 9732096
  11.1 5.8 %collective-permute-start.3 = (s32[256]{0:T(256)S(1)}, s32[256]{0:T(256)S(1)}, u32[]{:S(2)}, u32[]{:S(2)}) collective-permute-start(s32[256]{0:T(256)S(1)} %bitcast.52), channel_id=1, source_target_pairs={{0,24},{8,0},{16,8},{24,16},{1,25},{9,1},{17,9},{25,17},{2,26},{10... | collective-permute-start | bytes 3080 | tf_op jit(solution)/shard_map/ppermute | solution.py:83
  16.9 3.7 %collective-permute-start.4 = (s32[512]{0:T(512)S(1)}, s32[512]{0:T(512)S(1)}, u32[]{:S(2)}, u32[]{:S(2)}) collective-permute-start(s32[512]{0:T(512)S(1)} %pad_add_fusion), channel_id=1, source_target_pairs={{0,16},{8,24},{16,0},{24,8},{1,17},{9,25},{17,1},{25,9},{2,18},{10... | collective-permute-start | bytes 6152 | tf_op jit(solution)/shard_map/ppermute | solution.py:83
  115.1 12.4 %copy-start.1 = (bf16[256,768]{1,0:T(8,128)(2,1)S(1)}, bf16[256,768]{1,0:T(8,128)(2,1)}, u32[]{:S(2)}) copy-start(bf16[256,768]{1,0:T(8,128)(2,1)} %fusion.22) | copy-start | bytes 1179652
  115.2 11.8 %collective-permute-start = (bf16[256,768]{1,0:T(8,128)(2,1)S(1)}, bf16[256,768]{1,0:T(8,128)(2,1)S(1)}, u32[]{:S(2)}, u32[]{:S(2)}) collective-permute-start(bf16[256,768]{1,0:T(8,128)(2,1)S(1)} %multiply_convert_fusion.1), channel_id=1, source_target_pairs={{0,8},{8,16},{16,24},{24,0},{1,9},{9,17},{17,25},{25,1},{2,10},{10... | collective-permute-start | bytes 1179656 | tf_op jit(solution)/shard_map/ppermute | solution.py:12
  127.0 10.9 %collective-permute-start.1 = (bf16[256,768]{1,0:T(8,128)(2,1)S(1)}, bf16[256,768]{1,0:T(8,128)(2,1)S(1)}, u32[]{:S(2)}, u32[]{:S(2)}) collective-permute-start(bf16[256,768]{1,0:T(8,128)(2,1)S(1)} %collective-permute-done), channel_id=1, source_target_pairs={{0,8},{8,16},{16,24},{24,0},{1,9},{9,17},{17,25},{25,1},{2,10},{10... | collective-permute-start | bytes 1179656 | tf_op jit(solution)/shard_map/ppermute | solution.py:12
  137.8 10.0 %collective-permute-start.2 = (bf16[256,768]{1,0:T(8,128)(2,1)S(1)}, bf16[256,768]{1,0:T(8,128)(2,1)S(1)}, u32[]{:S(2)}, u32[]{:S(2)}) collective-permute-start(bf16[256,768]{1,0:T(8,128)(2,1)S(1)} %collective-permute-done.1), channel_id=1, source_target_pairs={{0,8},{8,16},{16,24},{24,0},{1,9},{9,17},{17,25},{25,1},{2,10},{10... | collective-permute-start | bytes 1179656 | tf_op jit(solution)/shard_map/ppermute | solution.py:12
  150.0 1.0 copy-start.2
Sparse Core Ops, SparseCore 0:
  9.7 54.3 all-gather.2
  66.5 29.7 all-gather.4
  115.3 135.6 reduce-scatter.3
